TPU v7x, 32 devices: a whole 2x2x4 slice. The times are simulated.
32 devices in a mesh: ctx: 4 (over y, x), tp: 8 (over z, core).
Axes of the slice: x: 2, y: 2, z: 4, core: 2. Of those that a mesh axis runs over, the one named last changes fastest.
Arguments:
- resid: bfloat16 [1024, 4096], P('ctx', 'tp'), may hold values from -6 to 6
- attn_gain: bfloat16 [4096], replicated, may hold values from 0.5 to 1.5
- mlp_gain: bfloat16 [4096], replicated, may hold values from 0.5 to 1.5
- w_query: bfloat16 [4096, 4096], P(None, 'tp'), may hold values from -0.09375 to 0.09375
- w_kv: bfloat16 [4096, 1024], P(None, 'tp'), may hold values from -0.09375 to 0.09375
- w_out: bfloat16 [4096, 4096], P('tp'), may hold values from -0.09375 to 0.09375
- w_gate: bfloat16 [4096, 11008], P(None, 'tp'), may hold values from -0.09375 to 0.09375
- w_up: bfloat16 [4096, 11008], P(None, 'tp'), may hold values from -0.09375 to 0.09375
- w_down: bfloat16 [11008, 4096], P('tp'), may hold values from -0.0546875 to 0.0546875
- kv_cache: bfloat16 [32, 128, 1024], P('ctx'), may hold values from -70 to 70
- cache_len: int32 [4], replicated, may hold values from 1 to 2048
- span_len: int32 [4], replicated, may hold values from 1 to 256
- slot_req: int32 [32], P('ctx'), may hold values from 0 to 4, as said below
- slot_blk: int32 [32], P('ctx'), may hold values from 0 to 15, as said below
Outputs:
- layer_out: bfloat16 [1024, 4096], P('ctx', 'tp')
- new_kv: bfloat16 [1024, 1024], P('ctx', 'tp')
Inputs may be any that keep to these rules, and one draw needn't show every extreme that they name: `slot_req`: each request r holds ceil(cache_len[r] / 128) blocks, and each of its blocks stands in exactly one slot; every other slot is empty. `slot_blk`: block numbers of live slots are below their request's block count; empty slots carry 0.
All inputs are finite; a program needn't handle non-finite values.
Results may differ from a plain program's by a relative error of at most 0.035.
Values may be sent and summed in bfloat16 or wider, within the bound.
No kernel may reach another device: no remote copies, remote signals or barrier semaphores. Data moves between devices by JAX's collectives and lax.ppermute only.
A program may use at most 128 MiB of HBM per device.

v0:
```python
import jax
import jax.numpy as jnp
from jax import lax
from jax.sharding import PartitionSpec as P

HQ = 32
KVH = 4
HD = 128
BLK = 128
THETA = 5000000.0
EPS = 1e-05
NEG = -1e30


def rms_norm(values, gain):
    wide = values.astype(jnp.float32)
    factor = lax.rsqrt(jnp.mean(wide * wide, axis=-1, keepdims=True) + EPS)
    return (wide * factor * gain.astype(jnp.float32)).astype(jnp.bfloat16)


def rotate(vectors, positions):
    width = vectors.shape[-1]
    half = width // 2
    freqs = THETA ** (-(jnp.arange(half, dtype=jnp.float32) * 2.0 / width))
    angles = positions.astype(jnp.float32)[:, None] * freqs[None, :]
    cosine = jnp.cos(angles)[:, None, :]
    sine = jnp.sin(angles)[:, None, :]
    first = vectors[..., :half]
    second = vectors[..., half:]
    return jnp.concatenate(
        [first * cosine - second * sine, second * cosine + first * sine], axis=-1
    )


def column_term(rows, weight):
    return lax.dot_general(
        weight, rows, (((0,), (1,)), ((), ())), preferred_element_type=jnp.float32
    )


def gather_ctx(value, count):
    parts = [value]
    for shift in range(1, count):
        pairs = [(i, (i + shift) % count) for i in range(count)]
        parts.append(lax.ppermute(value, "ctx", pairs))
    return parts


def per_device(
    resid,
    attn_gain,
    mlp_gain,
    w_query,
    w_kv,
    w_out,
    w_gate,
    w_up,
    w_down,
    kv_cache,
    cache_len,
    span_len,
    slot_req,
    slot_blk,
):
    span_size = resid.shape[0]
    ctx_count = lax.axis_size("ctx")
    q_cols = w_query.shape[1]
    heads_dev = q_cols // HD
    ctx_rank = lax.axis_index("ctx")
    tp_rank = lax.axis_index("tp")
    group = tp_rank * heads_dev // (HQ // KVH)
    my_len = cache_len[ctx_rank]
    my_span = span_len[ctx_rank]
    offsets = jnp.arange(span_size, dtype=jnp.int32)
    positions = my_len + offsets
    live_rows = offsets < my_span
    own_cache = jnp.concatenate(
        [
            lax.dynamic_slice_in_dim(kv_cache, group * HD, HD, 2),
            lax.dynamic_slice_in_dim(kv_cache, KVH * HD + group * HD, HD, 2),
        ],
        axis=2,
    )
    own_meta = jnp.stack([slot_req, slot_blk])
    cache_all = jnp.concatenate(gather_ctx(own_cache, ctx_count), axis=0)
    meta_all = jnp.concatenate(gather_ctx(own_meta, ctx_count), axis=1)
    full_resid = lax.all_gather(resid, "tp", axis=1, tiled=True)
    x_norm = rms_norm(full_resid, attn_gain)
    query = rotate(
        jnp.dot(x_norm, w_query, preferred_element_type=jnp.float32).reshape(
            span_size, heads_dev, HD
        ),
        positions,
    ).astype(jnp.bfloat16)
    kv_piece = jnp.dot(x_norm, w_kv, preferred_element_type=jnp.float32).astype(jnp.bfloat16)
    kv_width = kv_piece.shape[1]
    kv_all = lax.all_gather(kv_piece, "tp", axis=1, tiled=True)
    all_keys = rotate(
        kv_all[:, : KVH * HD].astype(jnp.float32).reshape(span_size, KVH, HD), positions
    ).astype(jnp.bfloat16)
    joined = jnp.concatenate([all_keys.reshape(span_size, KVH * HD), kv_all[:, KVH * HD :]], axis=1)
    mine = lax.dynamic_slice_in_dim(joined, tp_rank * kv_width, kv_width, 1)
    new_kv = jnp.where(live_rows[:, None], mine, jnp.zeros_like(mine))
    new_keys = lax.dynamic_index_in_dim(all_keys, group, 1, keepdims=False)
    new_vals = lax.dynamic_slice_in_dim(kv_all, KVH * HD + group * HD, HD, 1)
    cache_rows = cache_all.shape[0] * BLK
    keys = jnp.concatenate([cache_all[..., :HD].reshape(cache_rows, HD), new_keys], axis=0)
    vals = jnp.concatenate([cache_all[..., HD:].reshape(cache_rows, HD), new_vals], axis=0)
    key_pos = meta_all[1][:, None] * BLK + jnp.arange(BLK, dtype=jnp.int32)[None, :]
    cache_ok = ((meta_all[0][:, None] == ctx_rank) & (key_pos < my_len)).reshape(cache_rows)
    new_ok = (offsets[None, :] <= offsets[:, None]) & (offsets[None, :] < my_span)
    valid = jnp.concatenate(
        [jnp.broadcast_to(cache_ok[None, :], (span_size, cache_rows)), new_ok], axis=1
    )
    scores = jnp.einsum("chd,kd->hck", query, keys, preferred_element_type=jnp.float32) * HD ** (
        -0.5
    )
    peak = jnp.max(jnp.where(valid[None], scores, NEG), axis=2)
    weights = jnp.where(valid[None], jnp.exp(scores - peak[..., None]), 0.0)
    total = jnp.sum(weights, axis=2)
    summed = jnp.einsum(
        "hck,kd->hcd", weights.astype(jnp.bfloat16), vals, preferred_element_type=jnp.float32
    )
    attn_rows = (
        (summed / total[..., None])
        .transpose(1, 0, 2)
        .reshape(span_size, q_cols)
        .astype(jnp.bfloat16)
    )
    head_sum = lax.psum_scatter(
        column_term(attn_rows, w_out).astype(jnp.bfloat16), "tp", scatter_dimension=0, tiled=True
    ).astype(jnp.float32)
    mid = (resid.astype(jnp.float32) + head_sum.T).astype(jnp.bfloat16)
    full_mid = lax.all_gather(mid, "tp", axis=1, tiled=True)
    x_two = rms_norm(full_mid, mlp_gain)
    gate = jnp.dot(x_two, w_gate, preferred_element_type=jnp.float32)
    up_part = jnp.dot(x_two, w_up, preferred_element_type=jnp.float32)
    hidden = (jax.nn.silu(gate) * up_part).astype(jnp.bfloat16)
    down_sum = lax.psum_scatter(
        column_term(hidden, w_down).astype(jnp.bfloat16), "tp", scatter_dimension=0, tiled=True
    ).astype(jnp.float32)
    layer_out = (mid.astype(jnp.float32) + down_sum.T).astype(jnp.bfloat16)
    layer_out = jnp.where(live_rows[:, None], layer_out, jnp.zeros_like(layer_out))
    return (layer_out, new_kv)


def solution(mesh):
    return jax.shard_map(
        per_device,
        mesh=mesh,
        in_specs=(
            P("ctx", "tp"),
            P(),
            P(),
            P(None, "tp"),
            P(None, "tp"),
            P("tp", None),
            P(None, "tp"),
            P(None, "tp"),
            P("tp", None),
            P("ctx", None, None),
            P(),
            P(),
            P("ctx"),
            P("ctx"),
        ),
        out_specs=(P("ctx", "tp"), P("ctx", "tp")),
        check_vma=False,
    )
```

profile of v0, /device:TPU:0, one launch (start us, length us, event | category | flops | bytes accessed | tf_op | source)
XLA Modules:
  0.0 242.1 jit_solution(6783432989193067769)
XLA Ops:
  8.6 3.9 %collective-permute-start.2 = (s32[2,8]{1,0:T(2,128)S(1)}, s32[2,8]{1,0:T(2,128)S(1)}, u32[]{:S(2)}, u32[]{:S(2)}) collective-permute-start(s32[2,8]{1,0:T(2,128)S(1)} %pad_add_fusion.1), channel_id=1, source_target_pairs={{0,24},{8,0},{16,8},{24,16},{1,25},{9,1},{17,9},{25,17},{2,26},{10... | collective-permute-start | bytes 200 | tf_op jit(solution)/shard_map/ppermute | solution.py:45
  14.8 2.4 collective-permute-start.5
  17.2 1.5 collective-permute-start.4
  18.7 1.2 dynamic_slice.22
  19.9 1.3 dynamic_slice.23
  25.5 5.1 %pad_add_fusion = pred[256,4352]{0,1:T(8,128)(4,1)} fusion(pred[256,256]{0,1:T(8,128)(4,1)S(1)} %fusion.46, pred[4352]{0:T(1024)(128)(4,1)S(1)} %pad.8.clone), kind=kLoop, calls=%fused_computation.20 | loop fusion | flops 1114112 | bytes 1184000 | tf_op jit(solution)/shard_map/concatenate | solution.py:112
  30.6 10.4 %collective-permute-done.4 = bf16[8,128,256]{2,1,0:T(8,128)(2,1)S(1)} collective-permute-done((bf16[8,128,256]{2,1,0:T(8,128)(2,1)S(1)}, bf16[8,128,256]{2,1,0:T(8,128)(2,1)S(1)}, u32[]{:S(2)}, u32[]{:S(2)}) %collective-permute-start.4) | collective-permute-done | bytes 524320 | tf_op jit(solution)/shard_map/ppermute | solution.py:45
  41.8 1.3 copy.25
  43.1 2.2 fusion.12
  45.4 2.6 %convolution_convert_fusion.2 = bf16[256,128]{1,0:T(8,128)(2,1)S(1)} fusion(bf16[4096,128]{1,0:T(8,128)(2,1)S(1)} %copy-done, bf16[256,4096]{1,0:T(8,128)(2,1)} %all-gather.3.cloned.1.call-done, f32[4096]{0:T(1024)S(1)} %convert_element_type.78, f32[256]{0:T(256)S(1)} %add_rsqrt_fusion.1), kind=kOutput, calls=%fused_computation.33 | convolution fusion | flops 272662528 | bytes 3228672 | tf_op jit(solution)/shard_map/dot_general | solution.py:95
  48.0 14.3 %all_gather.10 = bf16[256,1024]{1,0:T(8,128)(2,1)S(1)} all-gather(bf16[256,128]{1,0:T(8,128)(2,1)S(1)} %convolution_convert_fusion.2), channel_id=1, replica_groups=mesh['ctx'=4,'tp'=8] {'tp'}, dimensions={1}, use_global_device_ids=true | all-gather | bytes 589824 | tf_op jit(solution)/shard_map/all_gather | solution.py:97
  62.4 1.3 fusion.37
  65.3 8.7 %fusion.30 = f32[4352,256,4]{1,0,2:T(8,128)} fusion(bf16[256,128]{1,0:T(8,128)(2,1)S(1)} %dynamic-slice_bitcast_fusion, bf16[4096,128]{1,0:T(8,128)(2,1)S(1)} %bitcast.69, bf16[256,4,64]{2,0,1:T(8,128)(2,1)S(1)} %get-tuple-element.7, bf16[256,4,64]{2,0,1:T(8,128)(2,1)S(1)} %get-tuple-element.6), kind=kOutput, calls=%fused_computation.38 | convolution fusion | flops 1143603200 | bytes 19202048 | tf_op jit(solution)/shard_map/chd,kd->hck/dot_general | solution.py:115
  74.0 18.6 %fusion.60 = (f32[4,256]{1,0:T(4,128)S(1)}, bf16[4,256,4352]{1,2,0:T(8,128)(2,1)}) fusion(f32[4352,256,4]{1,0,2:T(8,128)} %fusion.30, pred[256,4352]{0,1:T(8,128)(4,1)} %pad_add_fusion), kind=kOutput, calls=%fused_computation.92 | output fusion | flops 31199488 | bytes 27856896 | tf_op jit(solution)/shard_map/sub | solution.py:119
  92.6 5.0 %fusion.25 = bf16[256,4,128]{0,2,1:T(8,128)(2,1)S(1)} fusion(bf16[4,256,4352]{1,2,0:T(8,128)(2,1)} %get-tuple-element.19, bf16[256,128]{0,1:T(8,128)(2,1)S(1)} %copy.21, bf16[4096,128]{0,1:T(8,128)(2,1)S(1)} %copy-done.6, f32[256,4]{0,1:T(4,128)S(1)} %bitcast.76), kind=kOutput, calls=%fused_computation.32 | convolution fusion | flops 1143341056 | bytes 10293248 | tf_op jit(solution)/shard_map/hck,kd->hcd/dot_general | solution.py:121
  97.7 2.7 %fusion.11 = bf16[4096,256]{0,1:T(8,128)(2,1)} fusion(bf16[256,512]{0,1:T(8,128)(2,1)S(1)} %bitcast.71, bf16[512,4096]{1,0:T(8,128)(2,1)S(1)} %copy-done.2), kind=kOutput, calls=%fused_computation.19 | convolution fusion | flops 1074790400 | bytes 6553600 | tf_op jit(solution)/shard_map/dot_general | solution.py:36
  100.4 34.6 %reduce-scatter.3.cloned.1.call-done = bf16[512,256]{0,1:T(8,128)(2,1)} async-done(((bf16[4096,256]{0,1:T(8,128)(2,1)}), bf16[512,256]{0,1:T(8,128)(2,1)}) %reduce-scatter.3.cloned.1.call-update) | async-done | bytes 262160 | tf_op jit(solution)/shard_map/reduce_scatter | solution.py:130
  135.0 1.7 fusion.41
  137.1 27.9 %all-gather.5.cloned.1.call-done = bf16[256,4096]{1,0:T(8,128)(2,1)} async-done(((bf16[256,512]{1,0:T(8,128)(2,1)}), bf16[256,4096]{1,0:T(8,128)(2,1)}) %all-gather.5.cloned.1.call-update) | async-done | bytes 2097168 | tf_op jit(solution)/shard_map/all_gather | solution.py:134
  164.9 2.1 fusion.15
  167.0 9.2 %fusion.35 = f32[256,1376]{0,1:T(8,128)} fusion(bf16[4096,1376]{0,1:T(8,128)(2,1)} %param.20, bf16[256,4096]{1,0:T(8,128)(2,1)} %all-gather.5.cloned.1.call-done, f32[4096]{0:T(1024)S(1)} %convert_element_type.91, f32[256]{0:T(256)S(1)} %add_rsqrt_fusion), kind=kOutput, calls=%fused_computation.41 | convolution fusion | flops 2889875456 | bytes 14795776 | tf_op jit(solution)/shard_map/dot_general | solution.py:136
  176.2 22.1 %fusion.10 = bf16[4096,256]{0,1:T(8,128)(2,1)} fusion(bf16[1376,4096]{1,0:T(8,128)(2,1)} %param.22, bf16[4096,1376]{0,1:T(8,128)(2,1)} %param.21, f32[256,1376]{0,1:T(8,128)} %fusion.35, bf16[256,4096]{1,0:T(8,128)(2,1)} %all-gather.5.cloned.1.call-done, f32[4096]{0:T(1024)S(1)} %convert_element_type.91, f32[256]{0:T(256)S(1)} %add_rsqrt_fusion), kind=kOutput, calls=%fused_computation.18 | convolution fusion | flops 5778718720 | bytes 28165120 | tf_op jit(solution)/shard_map/dot_general | solution.py:36
  199.3 34.6 %reduce-scatter.5.cloned.1.call-done = bf16[512,256]{0,1:T(8,128)(2,1)} async-done(((bf16[4096,256]{0,1:T(8,128)(2,1)}), bf16[512,256]{0,1:T(8,128)(2,1)}) %reduce-scatter.5.cloned.1.call-update) | async-done | bytes 262160 | tf_op jit(solution)/shard_map/reduce_scatter | solution.py:139
  233.8 1.8 fusion.42
  (67 shorter events, 11.7 us)
Async XLA Ops:
  7.2 38.2 %copy-start = (bf16[4096,128]{1,0:T(8,128)(2,1)S(1)}, bf16[4096,128]{1,0:T(8,128)(2,1)}, u32[]{:S(2)}) copy-start(bf16[4096,128]{1,0:T(8,128)(2,1)} %param.18) | copy-start | bytes 3145732
  7.2 36.0 %all-gather.3.cloned.1.call-start = ((), (), s32[]{:S(2)}) async-start(), calls=%async_computation.2 | async-start | bytes 2359296 | tf_op jit(solution)/shard_map/all_gather | solution.py:87
  7.9 127.1 %reduce-scatter.3.cloned.1.call-start = ((), (), s32[]{:S(2)}) async-start(), calls=%async_computation.3 | async-start | bytes 2359296 | tf_op jit(solution)/shard_map/reduce_scatter | solution.py:130
  8.6 15.2 %collective-permute-start.2 = (s32[2,8]{1,0:T(2,128)S(1)}, s32[2,8]{1,0:T(2,128)S(1)}, u32[]{:S(2)}, u32[]{:S(2)}) collective-permute-start(s32[2,8]{1,0:T(2,128)S(1)} %pad_add_fusion.1), channel_id=1, source_target_pairs={{0,24},{8,0},{16,8},{24,16},{1,25},{9,1},{17,9},{25,17},{2,26},{10... | collective-permute-start | bytes 200 | tf_op jit(solution)/shard_map/ppermute | solution.py:45
  12.5 11.4 %collective-permute-start.1 = (s32[2,8]{1,0:T(2,128)S(1)}, s32[2,8]{1,0:T(2,128)S(1)}, u32[]{:S(2)}, u32[]{:S(2)}) collective-permute-start(s32[2,8]{1,0:T(2,128)S(1)} %pad_add_fusion.1), channel_id=1, source_target_pairs={{0,16},{8,24},{16,0},{24,8},{1,17},{9,25},{17,1},{25,9},{2,18},{10... | collective-permute-start | bytes 200 | tf_op jit(solution)/shard_map/ppermute | solution.py:45
  13.0 10.9 %collective-permute-start = (s32[2,8]{1,0:T(2,128)S(1)}, s32[2,8]{1,0:T(2,128)S(1)}, u32[]{:S(2)}, u32[]{:S(2)}) collective-permute-start(s32[2,8]{1,0:T(2,128)S(1)} %pad_add_fusion.1), channel_id=1, source_target_pairs={{0,8},{8,16},{16,24},{24,0},{1,9},{9,17},{17,25},{25,1},{2,10},{10... | collective-permute-start | bytes 200 | tf_op jit(solution)/shard_map/ppermute | solution.py:45
  14.8 15.8 %collective-permute-start.5 = (bf16[8,128,256]{2,1,0:T(8,128)(2,1)S(1)}, bf16[8,128,256]{2,1,0:T(8,128)(2,1)S(1)}, u32[]{:S(2)}, u32[]{:S(2)}) collective-permute-start(bf16[8,128,256]{2,1,0:T(8,128)(2,1)S(1)} %pad_maximum_fusion.1), channel_id=1, source_target_pairs={{0,24},{8,0},{16,8},{24,16},{1,25},{9,1},{17,9},{25,17},{2,26},{10... | collective-permute-start | bytes 1572872 | tf_op jit(solution)/shard_map/ppermute | solution.py:45
  17.2 23.8 %collective-permute-start.4 = (bf16[8,128,256]{2,1,0:T(8,128)(2,1)S(1)}, bf16[8,128,256]{2,1,0:T(8,128)(2,1)S(1)}, u32[]{:S(2)}, u32[]{:S(2)}) collective-permute-start(bf16[8,128,256]{2,1,0:T(8,128)(2,1)S(1)} %pad_maximum_fusion.1), channel_id=1, source_target_pairs={{0,16},{8,24},{16,0},{24,8},{1,17},{9,25},{17,1},{25,9},{2,18},{10... | collective-permute-start | bytes 1572872 | tf_op jit(solution)/shard_map/ppermute | solution.py:45
  23.9 17.1 %collective-permute-start.3 = (bf16[8,128,256]{2,1,0:T(8,128)(2,1)S(1)}, bf16[8,128,256]{2,1,0:T(8,128)(2,1)S(1)}, u32[]{:S(2)}, u32[]{:S(2)}) collective-permute-start(bf16[8,128,256]{2,1,0:T(8,128)(2,1)S(1)} %pad_maximum_fusion.1), channel_id=1, source_target_pairs={{0,8},{8,16},{16,24},{24,0},{1,9},{9,17},{17,25},{25,1},{2,10},{10... | collective-permute-start | bytes 1572872 | tf_op jit(solution)/shard_map/ppermute | solution.py:45
  43.1 19.2 %copy-start.4 = (bf16[256,4096]{1,0:T(8,128)(2,1)S(1)}, bf16[256,4096]{1,0:T(8,128)(2,1)}, u32[]{:S(2)}) copy-start(bf16[256,4096]{1,0:T(8,128)(2,1)} %all-gather.3.cloned.1.call-done) | copy-start | bytes 6291460
  43.1 19.2 %copy-start.8 = (bf16[4096,512]{1,0:T(8,128)(2,1)S(1)}, bf16[4096,512]{1,0:T(8,128)(2,1)}, u32[]{:S(2)}) copy-start(bf16[4096,512]{1,0:T(8,128)(2,1)} %param.17) | copy-start | bytes 12582916
  74.0 18.6 %copy-start.6 = (bf16[4096,128]{0,1:T(8,128)(2,1)S(1)}, bf16[4096,128]{0,1:T(8,128)(2,1)}, u32[]{:S(2)}) copy-start(bf16[4096,128]{0,1:T(8,128)(2,1)} %copy.25) | copy-start | bytes 3145732
  92.6 5.0 %copy-start.2 = (bf16[512,4096]{1,0:T(8,128)(2,1)S(1)}, bf16[512,4096]{1,0:T(8,128)(2,1)}, u32[]{:S(2)}) copy-start(bf16[512,4096]{1,0:T(8,128)(2,1)} %param.19) | copy-start | bytes 12582916
  97.6 37.4 %copy-start.5 = (bf16[256,512]{1,0:T(8,128)(2,1)S(1)}, bf16[256,512]{1,0:T(8,128)(2,1)}, u32[]{:S(2)}) copy-start(bf16[256,512]{1,0:T(8,128)(2,1)} %param.14) | copy-start | bytes 786436
  97.6 39.4 %copy-start.7 = (bf16[4096]{0:T(1024)(128)(2,1)S(1)}, bf16[4096]{0:T(1024)(128)(2,1)}, u32[]{:S(2)}) copy-start(bf16[4096]{0:T(1024)(128)(2,1)} %param.16) | copy-start | bytes 24580
  100.3 64.6 %all-gather.5.cloned.1.call-start = ((), (), s32[]{:S(2)}) async-start(), calls=%async_computation.4 | async-start | bytes 2359296 | tf_op jit(solution)/shard_map/all_gather | solution.py:134
  136.8 97.0 %reduce-scatter.5.cloned.1.call-start = ((), (), s32[]{:S(2)}) async-start(), calls=%async_computation.5 | async-start | bytes 2359296 | tf_op jit(solution)/shard_map/reduce_scatter | solution.py:139
  176.2 57.6 %copy-start.3 = (bf16[256,512]{1,0:T(8,128)(2,1)S(1)}, bf16[256,512]{1,0:T(8,128)(2,1)}, u32[]{:S(2)}) copy-start(bf16[256,512]{1,0:T(8,128)(2,1)} %fusion.41) | copy-start | bytes 786436
  176.2 59.4 %copy-start.1 = (bf16[4096,128]{1,0:T(8,128)(2,1)S(1)}, bf16[4096,128]{1,0:T(8,128)(2,1)}, u32[]{:S(2)}) copy-start(bf16[4096,128]{1,0:T(8,128)(2,1)} %param.18) | copy-start | bytes 3145732
Sparse Core Ops, SparseCore 0:
  9.6 31.7 all-gather.2
  100.4 34.5 reduce-scatter.2
  137.2 27.6 all-gather.4
  198.5 35.2 reduce-scatter.4
where the time goes:
time: 242 us
  waiting for transfers between devices  108 us (45%)
  matrix products  51.5 us (21%)
  other arithmetic  38 us (16%)
  blocking collectives  14.3 us (6%)
  between operations  14 us (6%)
  starting transfers between devices  9.33 us (4%)
  local copies, waits for them, and re-layouts  6.72 us (3%)
    reduce_scatter x1, waiting for transfers between devices, per_device(): lax.psum_scatter(column_term(attn_rows, w_out).astype(jnp.bfloat16), 'tp'...  34.6 us
    reduce_scatter x1, waiting for transfers between devices, per_device(): lax.psum_scatter(column_term(hidden, w_down).astype(jnp.bfloat16), 'tp',...  34.6 us
    all_gather x1, waiting for transfers between devices, per_device(): full_mid = lax.all_gather(mid, 'tp', axis=1, tiled=True)  27.9 us
    dot_general x2, matrix products, column_term(): lax.dot_general(weight, rows, (((0,), (1,)), ((), ())), preferred_element...  24.8 us
    sub x1, other arithmetic, per_device(): weights = jnp.where(valid[None], jnp.exp(scores - peak[..., None]), 0.0)  18.6 us
    all_gather x1, blocking collectives, per_device(): kv_all = lax.all_gather(kv_piece, 'tp', axis=1, tiled=True)  14.3 us
    ppermute x6, waiting for transfers between devices, gather_ctx(): parts.append(lax.ppermute(value, 'ctx', pairs))  10.4 us
    dot_general x1, matrix products, per_device(): gate = jnp.dot(x_two, w_gate, preferred_element_type=jnp.float32)  9.17 us
  transfers between devices with their start and end apart: 10, of which 4 were waited for; matrix products, arithmetic and copies ran while one was open for 7% of the time, Pallas kernels for 0%

commit v1 on v0

--- a/solution.py
+++ b/solution.py
@@ -10,6 +10,25 @@
 THETA = 5000000.0
 EPS = 1e-05
 NEG = -1e30
+
+
+def assign_plane_now(x0):
+    lane_axis = "tp"
+    b_next, all_values, d_next = (lax.axis_size(lane_axis), lax.axis_index(lane_axis), x0.shape[1])
+    mid_arr, k_now = (x0, 1)
+    while k_now < b_next:
+        mid_arr = jnp.concatenate(
+            [
+                mid_arr,
+                lax.ppermute(
+                    mid_arr, lane_axis, [(it, (it - k_now) % b_next) for it in range(b_next)]
+                ),
+            ],
+            axis=1,
+        )
+        k_now = 2 * k_now
+    v_next = jnp.roll(mid_arr, all_values * d_next, axis=1)
+    return v_next
 
 
 def rms_norm(values, gain):
@@ -131,7 +150,7 @@
         column_term(attn_rows, w_out).astype(jnp.bfloat16), "tp", scatter_dimension=0, tiled=True
     ).astype(jnp.float32)
     mid = (resid.astype(jnp.float32) + head_sum.T).astype(jnp.bfloat16)
-    full_mid = lax.all_gather(mid, "tp", axis=1, tiled=True)
+    full_mid = assign_plane_now(mid)
     x_two = rms_norm(full_mid, mlp_gain)
     gate = jnp.dot(x_two, w_gate, preferred_element_type=jnp.float32)
     up_part = jnp.dot(x_two, w_up, preferred_element_type=jnp.float32)

time: 242 us -> 286 us (1.18)
  waiting for transfers between devices: 108 us -> 143 us
  local copies, waits for them, and re-layouts: 6.72 us -> 12.8 us
    ppermute x0 -> x3, waiting for transfers between devices: none -> 63.1 us  [assign_plane_now(): lax.ppermute(mid_arr, lane_axis, [(it, (it - k_now) % b_next) for it in r...]
    all_gather x1 -> x0, waiting for transfers between devices: 27.9 us -> none  [per_device(): full_mid = lax.all_gather(mid, 'tp', axis=1, tiled=True)]
    unnamed x18 -> x24, local copies, waits for them, and re-layouts: 0.05 us -> 5.12 us
  transfers between devices with their start and end apart: 10 -> 12, of which waited for: 4 -> 6; matrix products, arithmetic and copies ran while one was open for 7% -> 6% of each run, Pallas kernels for 0% -> 0%
where the time goes in v1:
time: 286 us
  waiting for transfers between devices  143 us (50%)
  matrix products  51.8 us (18%)
  other arithmetic  39.9 us (14%)
  blocking collectives  14.3 us (5%)
  between operations  14 us (5%)
  local copies, waits for them, and re-layouts  12.8 us (4%)
  starting transfers between devices  10.4 us (4%)
    ppermute x3, waiting for transfers between devices, assign_plane_now(): lax.ppermute(mid_arr, lane_axis, [(it, (it - k_now) % b_next) for it in r...  63.1 us
    reduce_scatter x1, waiting for transfers between devices, per_device(): lax.psum_scatter(column_term(attn_rows, w_out).astype(jnp.bfloat16), 'tp'...  34.7 us
    reduce_scatter x1, waiting for transfers between devices, per_device(): lax.psum_scatter(column_term(hidden, w_down).astype(jnp.bfloat16), 'tp',...  33.8 us
    dot_general x2, matrix products, column_term(): lax.dot_general(weight, rows, (((0,), (1,)), ((), ())), preferred_element...  25.1 us
    sub x1, other arithmetic, per_device(): weights = jnp.where(valid[None], jnp.exp(scores - peak[..., None]), 0.0)  18.6 us
    all_gather x1, blocking collectives, per_device(): kv_all = lax.all_gather(kv_piece, 'tp', axis=1, tiled=True)  14.3 us
    ppermute x6, waiting for transfers between devices, gather_ctx(): parts.append(lax.ppermute(value, 'ctx', pairs))  10.4 us
    dot_general x1, matrix products, per_device(): gate = jnp.dot(x_two, w_gate, preferred_element_type=jnp.float32)  9.14 us
  transfers between devices with their start and end apart: 12, of which 6 were waited for; matrix products, arithmetic and copies ran while one was open for 6% of the time, Pallas kernels for 0%

profile of v1, /device:TPU:0, one launch (start us, length us, event | category | flops | bytes accessed | tf_op | source)
XLA Modules:
  0.0 286.0 jit_solution(10277989123408768211)
XLA Ops:
  8.6 3.9 %collective-permute-start.2 = (s32[2,8]{1,0:T(2,128)S(1)}, s32[2,8]{1,0:T(2,128)S(1)}, u32[]{:S(2)}, u32[]{:S(2)}) collective-permute-start(s32[2,8]{1,0:T(2,128)S(1)} %pad_add_fusion.1), channel_id=1, source_target_pairs={{0,24},{8,0},{16,8},{24,16},{1,25},{9,1},{17,9},{25,17},{2,26},{10... | collective-permute-start | bytes 200 | tf_op jit(solution)/shard_map/ppermute | solution.py:64
  14.8 2.4 collective-permute-start.5
  17.2 1.5 collective-permute-start.4
  25.5 5.1 %pad_add_fusion = pred[256,4352]{0,1:T(8,128)(4,1)} fusion(pred[256,256]{0,1:T(8,128)(4,1)S(1)} %fusion.48, pred[4352]{0:T(1024)(128)(4,1)S(1)} %pad.13.clone), kind=kLoop, calls=%fused_computation.20 | loop fusion | flops 1114112 | bytes 1184000 | tf_op jit(solution)/shard_map/concatenate | solution.py:131
  30.6 10.4 %collective-permute-done.4 = bf16[8,128,256]{2,1,0:T(8,128)(2,1)S(1)} collective-permute-done((bf16[8,128,256]{2,1,0:T(8,128)(2,1)S(1)}, bf16[8,128,256]{2,1,0:T(8,128)(2,1)S(1)}, u32[]{:S(2)}, u32[]{:S(2)}) %collective-permute-start.4) | collective-permute-done | bytes 524320 | tf_op jit(solution)/shard_map/ppermute | solution.py:64
  41.8 1.3 copy.25
  43.1 2.2 fusion.12
  45.4 2.6 convolution_convert_fusion.2
  48.0 14.3 %all_gather.7 = bf16[256,1024]{1,0:T(8,128)(2,1)S(1)} all-gather(bf16[256,128]{1,0:T(8,128)(2,1)S(1)} %convolution_convert_fusion.2), channel_id=1, replica_groups=mesh['ctx'=4,'tp'=8] {'tp'}, dimensions={1}, use_global_device_ids=true | all-gather | bytes 589824 | tf_op jit(solution)/shard_map/all_gather | solution.py:116
  63.0 1.3 fusion.35
  66.0 8.7 %fusion.29 = f32[4352,256,4]{1,0,2:T(8,128)} fusion(bf16[256,128]{1,0:T(8,128)(2,1)S(1)} %dynamic-slice_bitcast_fusion, bf16[4096,128]{1,0:T(8,128)(2,1)S(1)} %bitcast.70, bf16[256,4,64]{2,0,1:T(8,128)(2,1)S(1)} %get-tuple-element.9, bf16[256,4,64]{2,0,1:T(8,128)(2,1)S(1)} %get-tuple-element.8), kind=kOutput, calls=%fused_computation.37 | convolution fusion | flops 1143603200 | bytes 19202048 | tf_op jit(solution)/shard_map/chd,kd->hck/dot_general | solution.py:134
  74.6 18.6 %fusion.66 = (f32[4,256]{1,0:T(4,128)S(1)}, bf16[4,256,4352]{1,2,0:T(8,128)(2,1)}) fusion(f32[4352,256,4]{1,0,2:T(8,128)} %fusion.29, pred[256,4352]{0,1:T(8,128)(4,1)} %pad_add_fusion), kind=kOutput, calls=%fused_computation.105 | output fusion | flops 31199488 | bytes 27856896 | tf_op jit(solution)/shard_map/sub | solution.py:138
  93.3 5.0 %fusion.24 = bf16[256,4,128]{0,2,1:T(8,128)(2,1)S(1)} fusion(bf16[4,256,4352]{1,2,0:T(8,128)(2,1)} %get-tuple-element.21, bf16[256,128]{0,1:T(8,128)(2,1)S(1)} %copy.21, bf16[4096,128]{0,1:T(8,128)(2,1)S(1)} %copy-done.5, f32[256,4]{0,1:T(4,128)S(1)} %bitcast.77), kind=kOutput, calls=%fused_computation.31 | convolution fusion | flops 1143341056 | bytes 10293248 | tf_op jit(solution)/shard_map/hck,kd->hcd/dot_general | solution.py:140
  98.3 2.7 fusion.11
  101.0 34.7 %reduce-scatter.3.cloned.1.call-done = bf16[512,256]{0,1:T(8,128)(2,1)} async-done(((bf16[4096,256]{0,1:T(8,128)(2,1)}), bf16[512,256]{0,1:T(8,128)(2,1)}) %reduce-scatter.3.cloned.1.call-update) | async-done | bytes 262160 | tf_op jit(solution)/shard_map/reduce_scatter | solution.py:149
  135.7 1.8 constant_dynamic-update-slice_fusion.7
  138.5 3.9 %collective-permute-done.6 = bf16[256,512]{1,0:T(8,128)(2,1)S(1)} collective-permute-done((bf16[256,512]{1,0:T(8,128)(2,1)S(1)}, bf16[256,512]{1,0:T(8,128)(2,1)S(1)}, u32[]{:S(2)}, u32[]{:S(2)}) %collective-permute-start.6) | collective-permute-done | bytes 262176 | tf_op jit(solution)/shard_map/ppermute | solution.py:23
  142.8 11.7 %collective-permute-done.7 = bf16[256,1024]{1,0:T(8,128)(2,1)S(1)} collective-permute-done((bf16[256,1024]{1,0:T(8,128)(2,1)S(1)}, bf16[256,1024]{1,0:T(8,128)(2,1)S(1)}, u32[]{:S(2)}, u32[]{:S(2)}) %collective-permute-start.7) | collective-permute-done | bytes 524320 | tf_op jit(solution)/shard_map/ppermute | solution.py:23
  157.2 47.5 %collective-permute-done.8 = bf16[256,2048]{1,0:T(8,128)(2,1)S(1)} collective-permute-done((bf16[256,2048]{1,0:T(8,128)(2,1)}, bf16[256,2048]{1,0:T(8,128)(2,1)S(1)}, u32[]{:S(2)}, u32[]{:S(2)}) %collective-permute-start.8) | collective-permute-done | bytes 1048608 | tf_op jit(solution)/shard_map/ppermute | solution.py:23
  209.3 2.1 fusion.15
  211.3 9.1 %fusion.42 = f32[256,1376]{0,1:T(8,128)} fusion(bf16[4096,1376]{0,1:T(8,128)(2,1)} %param.20, f32[4096]{0:T(1024)S(1)} %convert_element_type.91, f32[256]{0:T(256)S(1)} %add_rsqrt_fusion, bf16[256,8192]{1,0:T(8,128)(2,1)} %constant_dynamic-update-slice_fusion, s32[]{:T(128)S(6)} %select_n.58), kind=kOutput, calls=%fused_computation.57 | convolution fusion | flops 2889875456 | bytes 14795780 | tf_op jit(solution)/shard_map/dot_general | solution.py:155
  220.5 22.4 %fusion.10 = bf16[4096,256]{0,1:T(8,128)(2,1)} fusion(bf16[1376,4096]{1,0:T(8,128)(2,1)} %param.22, f32[256,1376]{0,1:T(8,128)} %fusion.42, bf16[4096,1376]{0,1:T(8,128)(2,1)} %param.21, f32[4096]{0:T(1024)S(1)} %convert_element_type.91, f32[256]{0:T(256)S(1)} %add_rsqrt_fusion, bf16[256,8192]{1,0:T(8,128)(2,1)} %constant_dynamic-update-slice_fusion, ...), kind=kOutput, calls=%fused_computation.18 | convolution fusion | flops 5778718720 | bytes 28165124 | tf_op jit(solution)/shard_map/dot_general | solution.py:55
  243.8 33.8 %reduce-scatter.5.cloned.1.call-done = bf16[512,256]{0,1:T(8,128)(2,1)} async-done(((bf16[4096,256]{0,1:T(8,128)(2,1)}), bf16[512,256]{0,1:T(8,128)(2,1)}) %reduce-scatter.5.cloned.1.call-update) | async-done | bytes 262160 | tf_op jit(solution)/shard_map/reduce_scatter | solution.py:158
  277.7 1.8 fusion.44
  (79 shorter events, 23.2 us)
Async XLA Ops:
  7.2 38.2 %copy-start = (bf16[4096,128]{1,0:T(8,128)(2,1)S(1)}, bf16[4096,128]{1,0:T(8,128)(2,1)}, u32[]{:S(2)}) copy-start(bf16[4096,128]{1,0:T(8,128)(2,1)} %param.18) | copy-start | bytes 3145732
  7.2 35.9 %all-gather.2.cloned.1.call-start = ((), (), s32[]{:S(2)}) async-start(), calls=%async_computation.2 | async-start | bytes 2359296 | tf_op jit(solution)/shard_map/all_gather | solution.py:106
  7.9 127.8 %reduce-scatter.3.cloned.1.call-start = ((), (), s32[]{:S(2)}) async-start(), calls=%async_computation.3 | async-start | bytes 2359296 | tf_op jit(solution)/shard_map/reduce_scatter | solution.py:149
  8.6 15.2 %collective-permute-start.2 = (s32[2,8]{1,0:T(2,128)S(1)}, s32[2,8]{1,0:T(2,128)S(1)}, u32[]{:S(2)}, u32[]{:S(2)}) collective-permute-start(s32[2,8]{1,0:T(2,128)S(1)} %pad_add_fusion.1), channel_id=1, source_target_pairs={{0,24},{8,0},{16,8},{24,16},{1,25},{9,1},{17,9},{25,17},{2,26},{10... | collective-permute-start | bytes 200 | tf_op jit(solution)/shard_map/ppermute | solution.py:64
  12.5 11.4 %collective-permute-start.1 = (s32[2,8]{1,0:T(2,128)S(1)}, s32[2,8]{1,0:T(2,128)S(1)}, u32[]{:S(2)}, u32[]{:S(2)}) collective-permute-start(s32[2,8]{1,0:T(2,128)S(1)} %pad_add_fusion.1), channel_id=1, source_target_pairs={{0,16},{8,24},{16,0},{24,8},{1,17},{9,25},{17,1},{25,9},{2,18},{10... | collective-permute-start | bytes 200 | tf_op jit(solution)/shard_map/ppermute | solution.py:64
  13.0 10.9 %collective-permute-start = (s32[2,8]{1,0:T(2,128)S(1)}, s32[2,8]{1,0:T(2,128)S(1)}, u32[]{:S(2)}, u32[]{:S(2)}) collective-permute-start(s32[2,8]{1,0:T(2,128)S(1)} %pad_add_fusion.1), channel_id=1, source_target_pairs={{0,8},{8,16},{16,24},{24,0},{1,9},{9,17},{17,25},{25,1},{2,10},{10... | collective-permute-start | bytes 200 | tf_op jit(solution)/shard_map/ppermute | solution.py:64
  14.8 15.8 %collective-permute-start.5 = (bf16[8,128,256]{2,1,0:T(8,128)(2,1)S(1)}, bf16[8,128,256]{2,1,0:T(8,128)(2,1)S(1)}, u32[]{:S(2)}, u32[]{:S(2)}) collective-permute-start(bf16[8,128,256]{2,1,0:T(8,128)(2,1)S(1)} %pad_maximum_fusion.2), channel_id=1, source_target_pairs={{0,24},{8,0},{16,8},{24,16},{1,25},{9,1},{17,9},{25,17},{2,26},{10... | collective-permute-start | bytes 1572872 | tf_op jit(solution)/shard_map/ppermute | solution.py:64
  17.2 23.8 %collective-permute-start.4 = (bf16[8,128,256]{2,1,0:T(8,128)(2,1)S(1)}, bf16[8,128,256]{2,1,0:T(8,128)(2,1)S(1)}, u32[]{:S(2)}, u32[]{:S(2)}) collective-permute-start(bf16[8,128,256]{2,1,0:T(8,128)(2,1)S(1)} %pad_maximum_fusion.2), channel_id=1, source_target_pairs={{0,16},{8,24},{16,0},{24,8},{1,17},{9,25},{17,1},{25,9},{2,18},{10... | collective-permute-start | bytes 1572872 | tf_op jit(solution)/shard_map/ppermute | solution.py:64
  23.9 17.1 %collective-permute-start.3 = (bf16[8,128,256]{2,1,0:T(8,128)(2,1)S(1)}, bf16[8,128,256]{2,1,0:T(8,128)(2,1)S(1)}, u32[]{:S(2)}, u32[]{:S(2)}) collective-permute-start(bf16[8,128,256]{2,1,0:T(8,128)(2,1)S(1)} %pad_maximum_fusion.2), channel_id=1, source_target_pairs={{0,8},{8,16},{16,24},{24,0},{1,9},{9,17},{17,25},{25,1},{2,10},{10... | collective-permute-start | bytes 1572872 | tf_op jit(solution)/shard_map/ppermute | solution.py:64
  43.1 19.9 %copy-start.3 = (bf16[256,4096]{1,0:T(8,128)(2,1)S(1)}, bf16[256,4096]{1,0:T(8,128)(2,1)}, u32[]{:S(2)}) copy-start(bf16[256,4096]{1,0:T(8,128)(2,1)} %all-gather.2.cloned.1.call-done) | copy-start | bytes 6291460
  43.1 19.9 %copy-start.8 = (bf16[4096,512]{1,0:T(8,128)(2,1)S(1)}, bf16[4096,512]{1,0:T(8,128)(2,1)}, u32[]{:S(2)}) copy-start(bf16[4096,512]{1,0:T(8,128)(2,1)} %param.17) | copy-start | bytes 12582916
  74.6 18.6 %copy-start.5 = (bf16[4096,128]{0,1:T(8,128)(2,1)S(1)}, bf16[4096,128]{0,1:T(8,128)(2,1)}, u32[]{:S(2)}) copy-start(bf16[4096,128]{0,1:T(8,128)(2,1)} %copy.25) | copy-start | bytes 3145732
  93.2 5.0 %copy-start.2 = (bf16[512,4096]{1,0:T(8,128)(2,1)S(1)}, bf16[512,4096]{1,0:T(8,128)(2,1)}, u32[]{:S(2)}) copy-start(bf16[512,4096]{1,0:T(8,128)(2,1)} %param.19) | copy-start | bytes 12582916
  98.3 37.4 %copy-start.6 = (bf16[256,512]{1,0:T(8,128)(2,1)S(1)}, bf16[256,512]{1,0:T(8,128)(2,1)}, u32[]{:S(2)}) copy-start(bf16[256,512]{1,0:T(8,128)(2,1)} %param.14) | copy-start | bytes 786436
  100.9 54.7 %copy-start.7 = (bf16[4096]{0:T(1024)(128)(2,1)S(1)}, bf16[4096]{0:T(1024)(128)(2,1)}, u32[]{:S(2)}) copy-start(bf16[4096]{0:T(1024)(128)(2,1)} %param.16) | copy-start | bytes 24580
  101.0 176.7 %reduce-scatter.5.cloned.1.call-start = ((), (), s32[]{:S(2)}) async-start(), calls=%async_computation.4 | async-start | bytes 2359296 | tf_op jit(solution)/shard_map/reduce_scatter | solution.py:158
  137.5 5.0 %collective-permute-start.6 = (bf16[256,512]{1,0:T(8,128)(2,1)S(1)}, bf16[256,512]{1,0:T(8,128)(2,1)S(1)}, u32[]{:S(2)}, u32[]{:S(2)}) collective-permute-start(bf16[256,512]{1,0:T(8,128)(2,1)S(1)} %get-tuple-element.3), channel_id=1, source_target_pairs={{0,7},{1,0},{2,1},{3,2},{4,3},{5,4},{6,5},{7,6},{8,15},{9,8},{10,9... | collective-permute-start | bytes 786440 | tf_op jit(solution)/shard_map/ppermute | solution.py:23
  142.5 12.0 %collective-permute-start.7 = (bf16[256,1024]{1,0:T(8,128)(2,1)S(1)}, bf16[256,1024]{1,0:T(8,128)(2,1)S(1)}, u32[]{:S(2)}, u32[]{:S(2)}) collective-permute-start(bf16[256,1024]{1,0:T(8,128)(2,1)S(1)} %pad_maximum_fusion.3), channel_id=1, source_target_pairs={{0,6},{1,7},{2,0},{3,1},{4,2},{5,3},{6,4},{7,5},{8,14},{9,15},{10,... | collective-permute-start | bytes 1572872 | tf_op jit(solution)/shard_map/ppermute | solution.py:23
  155.6 49.1 %collective-permute-start.8 = (bf16[256,2048]{1,0:T(8,128)(2,1)}, bf16[256,2048]{1,0:T(8,128)(2,1)S(1)}, u32[]{:S(2)}, u32[]{:S(2)}) collective-permute-start(bf16[256,2048]{1,0:T(8,128)(2,1)} %pad_maximum_fusion.1), channel_id=1, source_target_pairs={{0,4},{1,5},{2,6},{3,7},{4,0},{5,1},{6,2},{7,3},{8,12},{9,13},{10,... | collective-permute-start | bytes 3145736 | tf_op jit(solution)/shard_map/ppermute | solution.py:23
  220.5 22.6 %copy-start.4 = (bf16[256,512]{1,0:T(8,128)(2,1)S(1)}, bf16[256,512]{1,0:T(8,128)(2,1)}, u32[]{:S(2)}) copy-start(bf16[256,512]{1,0:T(8,128)(2,1)} %get-tuple-element.12) | copy-start | bytes 786436
  220.5 58.9 %copy-start.1 = (bf16[4096,128]{1,0:T(8,128)(2,1)S(1)}, bf16[4096,128]{1,0:T(8,128)(2,1)}, u32[]{:S(2)}) copy-start(bf16[4096,128]{1,0:T(8,128)(2,1)} %param.18) | copy-start | bytes 3145732
Sparse Core Ops, SparseCore 0:
  9.6 31.7 all-gather.1
  101.1 34.5 reduce-scatter.2
  243.0 34.5 reduce-scatter.4
